TPU v7x, 256 devices: a whole 4x4x8 slice. The times are simulated.
256 devices in a mesh: rep: 32 (over z, y_hi, core), fsdp: 8 (over x, y_lo).
Axes of the slice: x: 4, y: 4 (y_hi: 2, y_lo: 2; y = y_hi * 2 + y_lo), z: 8, core: 2. Of those that a mesh axis runs over, the one named last changes fastest.
Arguments:
- hidden: bfloat16 [32768, 7168], P(('rep', 'fsdp')), may hold values from -6 to 6
- grad_out: bfloat16 [32768, 4096], P(('rep', 'fsdp')), may hold values from -24 to 24
- down_weight: bfloat16 [7168, 4096], P('fsdp'), may hold values from -0.0625 to 0.0625
- hash_tiles: bfloat16 [3, 32, 7168], P(None, None, 'fsdp'), may hold values from -1 to 1, as said below
- momentum: float32 [8, 3, 32, 4096], P('fsdp', None, None, 'rep'), may hold values from -6 to 6
- error: float32 [8, 3, 32, 4096], P('fsdp', None, None, 'rep'), may hold values from -6 to 6
Outputs:
- grad_hidden: bfloat16 [32768, 7168], P(('rep', 'fsdp'))
- update: float32 [7168, 4096], P('fsdp', 'rep')
- new_momentum: float32 [8, 3, 32, 4096], P('fsdp', None, None, 'rep')
- new_error: float32 [8, 3, 32, 4096], P('fsdp', None, None, 'rep')
Inputs may be any that keep to these rules, and one draw needn't show every extreme that they name: `hash_tiles`: in every sketch row each hidden unit has exactly one nonzero entry, +1 or -1, in one of the 32 buckets; all other entries are 0.
All inputs are finite; a program needn't handle non-finite values.
Results may differ from a plain program's by a relative error of at most 0.0005.
Values may be sent and summed in bfloat16 or wider, within the bound.
No kernel may reach another device: no remote copies, remote signals or barrier semaphores. Data moves between devices by JAX's collectives and lax.ppermute only.
A program may use at most 128 MiB of HBM per device.

v0:
```python
import math
import jax
import jax.numpy as jnp
from jax import lax
from jax.sharding import PartitionSpec as P

momentum_decay = 0.9
step_size = 0.5


def on_device(hidden, grad_out, down_weight, hash_tiles, momentum, error):
    shards = lax.axis_size("fsdp")
    replicas = lax.axis_size("rep")
    tok_rows = grad_out.shape[0]
    model_width = grad_out.shape[1]
    shard_rows = down_weight.shape[0]
    rows_count = hash_tiles.shape[0]
    buckets = hash_tiles.shape[1]
    sketch_rows = rows_count * buckets
    columns = model_width // replicas
    total_tokens = tok_rows * shards * replicas
    table_scale = math.sqrt(buckets / (shard_rows * total_tokens))
    gathered = lax.all_gather(grad_out, "fsdp", axis=0, tiled=True)
    partial_grads = lax.dot_general(
        gathered, down_weight, (((1,), (1,)), ((), ())), preferred_element_type=jnp.float32
    ).astype(jnp.bfloat16)
    grad_hidden = lax.all_to_all(partial_grads, "fsdp", split_axis=0, concat_axis=1, tiled=True)
    all_hash = lax.all_gather(hash_tiles, "fsdp", axis=2, tiled=True)
    projected = jnp.einsum(
        "kfi,tfi->fkt",
        all_hash.reshape(sketch_rows, shards, shard_rows),
        hidden.reshape(tok_rows, shards, shard_rows),
        preferred_element_type=jnp.float32,
    )
    received = lax.all_to_all(projected, "fsdp", split_axis=0, concat_axis=2, tiled=True)[0]
    split_grads = gathered.reshape(tok_rows * shards, replicas, columns)
    grad_block = split_grads.astype(jnp.float32)
    summed = jnp.einsum("kt,trc->rkc", received, grad_block, precision=lax.Precision.HIGHEST)
    sketch_table = lax.psum_scatter(
        (summed * table_scale).reshape(lax.axis_size("rep") * 1, rows_count, buckets, columns),
        "rep",
        scatter_dimension=0,
        tiled=True,
    )
    new_momentum = momentum_decay * momentum + sketch_table
    accumulated = error + step_size * new_momentum
    hash_float = hash_tiles.astype(jnp.float32)
    update = (
        jnp.einsum("jbi,jbc->ic", hash_float, accumulated[0], precision=lax.Precision.HIGHEST)
        / rows_count
    )
    encoded = jnp.einsum("jbi,ic->jbc", hash_float, update, precision=lax.Precision.HIGHEST)
    new_error = accumulated - encoded[None]
    return (grad_hidden, update, new_momentum, new_error)


def solution(mesh):
    return jax.shard_map(
        on_device,
        mesh=mesh,
        in_specs=(
            P(("rep", "fsdp"), None),
            P(("rep", "fsdp"), None),
            P("fsdp", None),
            P(None, None, "fsdp"),
            P("fsdp", None, None, "rep"),
            P("fsdp", None, None, "rep"),
        ),
        out_specs=(
            P(("rep", "fsdp"), None),
            P("fsdp", "rep"),
            P("fsdp", None, None, "rep"),
            P("fsdp", None, None, "rep"),
        ),
        check_vma=False,
    )
```

profile of v0, /device:TPU:2, one launch (start us, length us, event | category | flops | bytes accessed | tf_op | source)
XLA Modules:
  0.0 371.5 jit_solution(13918211053489265926)
XLA Ops:
  7.2 0.0 all-gather.5.cloned.1.call-start
  7.2 0.7 all-gather.5.cloned.1.call-update
  7.9 0.0 all-gather.3.cloned.1.call-start
  7.9 2.3 copy.13
  10.2 0.0 all-gather.3.cloned.1.call-update
  10.2 0.0 reduce-scatter.2.cloned.1.call-start
  10.3 46.5 %all-gather.5.cloned.1.call-done = bf16[3,32,7168]{2,1,0:T(8,128)(2,1)} async-done(((bf16[3,32,896]{2,1,0:T(8,128)(2,1)}), bf16[3,32,7168]{2,1,0:T(8,128)(2,1)}) %all-gather.5.cloned.1.call-update) | async-done | bytes 1376272 | tf_op jit(solution)/shard_map/all_gather | solution.py:28
  56.8 1.6 copy.23
  58.4 0.8 fusion
  59.1 10.5 %all_to_all.34 = f32[8,96,128]{2,1,0:T(8,128)S(1)} all-to-all(f32[8,96,128]{2,1,0:T(8,128)S(1)} %fusion), channel_id=1, replica_groups=mesh['rep'=32,'fsdp'=8] {'fsdp'}, dimensions={0} | all-to-all | bytes 786432 | tf_op jit(solution)/shard_map/all_to_all | solution.py:35
  69.6 0.2 copy.17
  69.9 0.1 reshape.28
  69.9 161.1 %all-gather.3.cloned.1.call-done = bf16[1024,4096]{0,1:T(8,128)(2,1)} async-done(((bf16[128,4096]{0,1:T(8,128)(2,1)}), bf16[1024,4096]{0,1:T(8,128)(2,1)}) %all-gather.3.cloned.1.call-update) | async-done | bytes 8388624 | tf_op jit(solution)/shard_map/all_gather | solution.py:23
  231.1 11.0 %convolution_multiply_fusion = f32[96,32,128]{2,0,1:T(8,128)} fusion(f32[96,1024,1]{1,0,2:T(8,128)S(1)} %reshape.28, bf16[1024,32,128]{0,2,1:T(8,128)(2,1)} %bitcast.43), kind=kOutput, calls=%fused_computation.4 | convolution fusion | flops 4832231424 | bytes 10354688 | tf_op jit(solution)/shard_map/kt,trc->rkc/dot_general | solution.py:38
  242.0 0.0 reduce-scatter.2.cloned.1.call-update
  242.1 13.5 %convolution_convert_fusion = bf16[1024,896]{1,0:T(8,128)(2,1)S(1)} fusion(bf16[1024,4096]{0,1:T(8,128)(2,1)} %all-gather.3.cloned.1.call-done, bf16[896,4096]{1,0:T(8,128)(2,1)} %param.8), kind=kOutput, calls=%fused_computation.3 | convolution fusion | flops 7517110272 | bytes 17563648 | tf_op jit(solution)/shard_map/dot_general | solution.py:24
  255.6 27.9 %all_to_all.35 = bf16[8,128,896]{2,1,0:T(8,128)(2,1)S(1)} all-to-all(bf16[8,128,896]{2,1,0:T(8,128)(2,1)S(1)} %bitcast.48), channel_id=1, replica_groups=mesh['rep'=32,'fsdp'=8] {'fsdp'}, dimensions={0} | all-to-all | bytes 3670016 | tf_op jit(solution)/shard_map/all_to_all | solution.py:27
  283.5 1.5 copy.22
  285.0 76.7 %reduce-scatter.2.cloned.1.call-done = f32[1,3,32,128]{3,2,1,0:T(8,128)} async-done(((f32[32,3,32,128]{3,2,1,0:T(8,128)}), f32[1,3,32,128]{3,2,1,0:T(8,128)}) %reduce-scatter.2.cloned.1.call-update) | async-done | bytes 49168 | tf_op jit(solution)/shard_map/reduce_scatter | solution.py:39
  361.7 0.8 multiply_add_fusion.1
  362.6 0.0 copy-start.1
  362.6 0.4 fusion.4
  363.0 1.0 fusion.5
  364.0 1.0 copy.19
  (9 shorter events, 0.0 us)
Async XLA Ops:
  7.2 49.6 %all-gather.5.cloned.1.call-start = ((), (), s32[]{:S(2)}) async-start(), calls=%async_computation.4 | async-start | bytes 1548288 | tf_op jit(solution)/shard_map/all_gather | solution.py:28
  7.9 223.2 %all-gather.3.cloned.1.call-start = ((), (), s32[]{:S(2)}) async-start(), calls=%async_computation.3 | async-start | bytes 9437184 | tf_op jit(solution)/shard_map/all_gather | solution.py:23
  10.2 48.1 %copy-start.4 = (bf16[128,7168]{1,0:T(8,128)(2,1)S(1)}, bf16[128,7168]{1,0:T(8,128)(2,1)}, u32[]{:S(2)}) copy-start(bf16[128,7168]{1,0:T(8,128)(2,1)} %param.6) | copy-start | bytes 5505028
  10.2 351.5 %reduce-scatter.2.cloned.1.call-start = ((), (), s32[]{:S(2)}) async-start(), calls=%async_computation.5 | async-start | bytes 1622016 | tf_op jit(solution)/shard_map/reduce_scatter | solution.py:39
  283.5 78.3 %copy-start.3 = (f32[1,3,32,128]{3,2,1,0:T(8,128)S(1)}, f32[1,3,32,128]{3,2,1,0:T(8,128)}, u32[]{:S(2)}) copy-start(f32[1,3,32,128]{3,2,1,0:T(8,128)} %param.10) | copy-start | bytes 147460
  283.5 79.1 %copy-start = (bf16[3,32,896]{2,1,0:T(8,128)(2,1)S(1)}, bf16[3,32,896]{2,1,0:T(8,128)(2,1)}, u32[]{:S(2)}) copy-start(bf16[3,32,896]{2,1,0:T(8,128)(2,1)} %param.9) | copy-start | bytes 516100
  283.5 79.1 %copy-start.2 = (f32[1,3,32,128]{3,2,1,0:T(8,128)S(1)}, f32[1,3,32,128]{3,2,1,0:T(8,128)}, u32[]{:S(2)}) copy-start(f32[1,3,32,128]{3,2,1,0:T(8,128)} %param.11) | copy-start | bytes 147460
  362.6 2.4 copy-start.1
Sparse Core Ops, SparseCore 0:
  9.8 46.9 all-gather.4
  59.1 171.9 all-gather.2
  242.2 119.5 reduce-scatter.1
where the time goes:
time: 372 us
  waiting for transfers between devices  285 us (77%)
  blocking collectives  38.4 us (10%)
  matrix products  26.7 us (7%)
  between operations  13.8 us (4%)
  local copies, waits for them, and re-layouts  6.63 us (2%)
    all_gather x1, waiting for transfers between devices, on_device(): gathered = lax.all_gather(grad_out, 'fsdp', axis=0, tiled=True)  161 us
    reduce_scatter x1, waiting for transfers between devices, on_device(): lax.psum_scatter((summed * table_scale).reshape(lax.axis_size('rep') * 1,...  76.7 us
    all_gather x1, waiting for transfers between devices, on_device(): all_hash = lax.all_gather(hash_tiles, 'fsdp', axis=2, tiled=True)  46.5 us
    all_to_all x1, blocking collectives, on_device(): lax.all_to_all(partial_grads, 'fsdp', split_axis=0, concat_axis=1, tiled=...  27.9 us
    dot_general x1, matrix products, on_device(): lax.dot_general(gathered, down_weight, (((1,), (1,)), ((), ())), preferre...  13.5 us
    dot_general x1, matrix products, on_device(): jnp.einsum('kt,trc->rkc', received, grad_block, precision=lax.Precision.H...  11 us
    all_to_all x1, blocking collectives, on_device(): lax.all_to_all(projected, 'fsdp', split_axis=0, concat_axis=2, tiled=True)  10.5 us
  transfers between devices with their start and end apart: 3, of which 3 were waited for; matrix products, arithmetic and copies ran while one was open for 5% of the time, Pallas kernels for 0%

commit v1 on v0

--- a/solution.py
+++ b/solution.py
@@ -25,7 +25,13 @@
         gathered, down_weight, (((1,), (1,)), ((), ())), preferred_element_type=jnp.float32
     ).astype(jnp.bfloat16)
     grad_hidden = lax.all_to_all(partial_grads, "fsdp", split_axis=0, concat_axis=1, tiled=True)
-    all_hash = lax.all_gather(hash_tiles, "fsdp", axis=2, tiled=True)
+    plain = lax.all_to_all(
+        jnp.stack(tuple((hash_tiles for _ in range(lax.axis_size("fsdp")))), axis=0),
+        axis_name="fsdp",
+        split_axis=0,
+        concat_axis=0,
+    )
+    all_hash = jnp.concatenate(plain, axis=2)
     projected = jnp.einsum(
         "kfi,tfi->fkt",
         all_hash.reshape(sketch_rows, shards, shard_rows),

time: 372 us -> 337 us (0.906)
  waiting for transfers between devices: 285 us -> 216 us
  blocking collectives: 38.4 us -> 73.9 us
    all_gather x1 -> x0, waiting for transfers between devices: 46.5 us -> none  [on_device(): all_hash = lax.all_gather(hash_tiles, 'fsdp', axis=2, tiled=True)]
    all_to_all x0 -> x1, blocking collectives: none -> 34.7 us  [on_device(): lax.all_to_all(jnp.stack(tuple((hash_tiles for _ in range(lax.axis_size('...]
    all_gather x1, waiting for transfers between devices: 161 us -> 138 us  [on_device(): gathered = lax.all_gather(grad_out, 'fsdp', axis=0, tiled=True)]
  transfers between devices with their start and end apart: 3 -> 2, of which waited for: 3 -> 2; matrix products, arithmetic and copies ran while one was open for 5% -> 5% of each run, Pallas kernels for 0% -> 0%
where the time goes in v1:
time: 337 us
  waiting for transfers between devices  216 us (64%)
  blocking collectives  73.9 us (22%)
  matrix products  26.7 us (8%)
  between operations  14.1 us (4%)
  local copies, waits for them, and re-layouts  5.2 us (2%)
    all_gather x1, waiting for transfers between devices, on_device(): gathered = lax.all_gather(grad_out, 'fsdp', axis=0, tiled=True)  138 us
    reduce_scatter x1, waiting for transfers between devices, on_device(): lax.psum_scatter((summed * table_scale).reshape(lax.axis_size('rep') * 1,...  78.1 us
    all_to_all x1, blocking collectives, on_device(): lax.all_to_all(jnp.stack(tuple((hash_tiles for _ in range(lax.axis_size('...  34.7 us
    all_to_all x1, blocking collectives, on_device(): lax.all_to_all(partial_grads, 'fsdp', split_axis=0, concat_axis=1, tiled=...  27.1 us
    dot_general x1, matrix products, on_device(): lax.dot_general(gathered, down_weight, (((1,), (1,)), ((), ())), preferre...  13.5 us
    all_to_all x1, blocking collectives, on_device(): lax.all_to_all(projected, 'fsdp', split_axis=0, concat_axis=2, tiled=True)  12.1 us
    dot_general x1, matrix products, on_device(): jnp.einsum('kt,trc->rkc', received, grad_block, precision=lax.Precision.H...  11 us
  transfers between devices with their start and end apart: 2, of which 2 were waited for; matrix products, arithmetic and copies ran while one was open for 5% of the time, Pallas kernels for 0%

profile of v1, /device:TPU:2, one launch (start us, length us, event | category | flops | bytes accessed | tf_op | source)
XLA Modules:
  0.0 336.7 jit_solution(13446011573906868605)
XLA Ops:
  7.2 0.0 all-gather.2.cloned.1.call-start
  7.2 2.3 copy.13
  9.5 0.0 all-gather.2.cloned.1.call-update
  9.5 0.0 copy-start.4
  9.6 0.0 reduce-scatter.2.cloned.1.call-start
  9.6 0.0 copy-done
  9.6 0.1 stack.2
  9.7 34.7 %all_to_all.39 = bf16[8,3,32,896]{3,2,1,0:T(8,128)(2,1)S(1)} all-to-all(bf16[8,3,32,896]{3,2,1,0:T(8,128)(2,1)S(1)} %stack.2), channel_id=1, replica_groups=mesh['rep'=32,'fsdp'=8] {'fsdp'}, dimensions={0} | all-to-all | bytes 2752512 | tf_op jit(solution)/shard_map/all_to_all | solution.py:28
  44.4 0.8 fusion
  45.2 12.1 %all_to_all.40 = f32[8,96,128]{2,1,0:T(8,128)S(1)} all-to-all(f32[8,96,128]{2,1,0:T(8,128)S(1)} %fusion), channel_id=1, replica_groups=mesh['rep'=32,'fsdp'=8] {'fsdp'}, dimensions={0} | all-to-all | bytes 786432 | tf_op jit(solution)/shard_map/all_to_all | solution.py:41
  57.3 0.2 copy.16
  57.5 0.1 reshape.30
  57.6 137.9 %all-gather.2.cloned.1.call-done = bf16[1024,4096]{0,1:T(8,128)(2,1)} async-done(((bf16[128,4096]{0,1:T(8,128)(2,1)}), bf16[1024,4096]{0,1:T(8,128)(2,1)}) %all-gather.2.cloned.1.call-update) | async-done | bytes 8388624 | tf_op jit(solution)/shard_map/all_gather | solution.py:23
  195.5 11.0 %convolution_multiply_fusion = f32[96,32,128]{2,0,1:T(8,128)} fusion(f32[96,1024,1]{1,0,2:T(8,128)S(1)} %reshape.30, bf16[1024,32,128]{0,2,1:T(8,128)(2,1)} %bitcast.44), kind=kOutput, calls=%fused_computation.4 | convolution fusion | flops 4832231424 | bytes 10354688 | tf_op jit(solution)/shard_map/kt,trc->rkc/dot_general | solution.py:44
  206.4 0.0 reduce-scatter.2.cloned.1.call-update
  206.5 13.5 %convolution_convert_fusion = bf16[1024,896]{1,0:T(8,128)(2,1)S(1)} fusion(bf16[1024,4096]{0,1:T(8,128)(2,1)} %all-gather.2.cloned.1.call-done, bf16[896,4096]{1,0:T(8,128)(2,1)} %param.8), kind=kOutput, calls=%fused_computation.3 | convolution fusion | flops 7517110272 | bytes 17563648 | tf_op jit(solution)/shard_map/dot_general | solution.py:24
  220.0 27.1 %all_to_all.41 = bf16[8,128,896]{2,1,0:T(8,128)(2,1)S(1)} all-to-all(bf16[8,128,896]{2,1,0:T(8,128)(2,1)S(1)} %bitcast.49), channel_id=1, replica_groups=mesh['rep'=32,'fsdp'=8] {'fsdp'}, dimensions={0} | all-to-all | bytes 3670016 | tf_op jit(solution)/shard_map/all_to_all | solution.py:27
  247.1 1.5 copy.21
  248.6 78.1 %reduce-scatter.2.cloned.1.call-done = f32[1,3,32,128]{3,2,1,0:T(8,128)} async-done(((f32[32,3,32,128]{3,2,1,0:T(8,128)}), f32[1,3,32,128]{3,2,1,0:T(8,128)}) %reduce-scatter.2.cloned.1.call-update) | async-done | bytes 49168 | tf_op jit(solution)/shard_map/reduce_scatter | solution.py:45
  326.7 0.8 multiply_add_fusion.1
  327.5 0.0 copy-start.1
  327.5 0.4 fusion.3
  327.9 1.0 fusion.4
  328.9 1.0 copy.18
  (7 shorter events, 0.0 us)
Async XLA Ops:
  7.2 2.4 copy-start
  7.2 188.3 %all-gather.2.cloned.1.call-start = ((), (), s32[]{:S(2)}) async-start(), calls=%async_computation.4 | async-start | bytes 9437184 | tf_op jit(solution)/shard_map/all_gather | solution.py:23
  9.5 34.9 %copy-start.4 = (bf16[128,7168]{1,0:T(8,128)(2,1)S(1)}, bf16[128,7168]{1,0:T(8,128)(2,1)}, u32[]{:S(2)}) copy-start(bf16[128,7168]{1,0:T(8,128)(2,1)} %param.6) | copy-start | bytes 5505028
  9.6 317.1 %reduce-scatter.2.cloned.1.call-start = ((), (), s32[]{:S(2)}) async-start(), calls=%async_computation.5 | async-start | bytes 1622016 | tf_op jit(solution)/shard_map/reduce_scatter | solution.py:45
  247.1 79.6 %copy-start.3 = (f32[1,3,32,128]{3,2,1,0:T(8,128)S(1)}, f32[1,3,32,128]{3,2,1,0:T(8,128)}, u32[]{:S(2)}) copy-start(f32[1,3,32,128]{3,2,1,0:T(8,128)} %param.10) | copy-start | bytes 147460
  247.1 80.4 %copy-start.2 = (f32[1,3,32,128]{3,2,1,0:T(8,128)S(1)}, f32[1,3,32,128]{3,2,1,0:T(8,128)}, u32[]{:S(2)}) copy-start(f32[1,3,32,128]{3,2,1,0:T(8,128)} %param.11) | copy-start | bytes 147460
  327.5 2.4 copy-start.1
Sparse Core Ops, SparseCore 0:
  10.3 185.1 all-gather.1
  206.6 120.0 reduce-scatter.1
